TPU v7x, 32 devices: a whole 2x2x4 slice. The times are simulated.
32 devices in a mesh: dp: 8 (over y, x, core), tensor: 4 (over z).
Axes of the slice: x: 2, y: 2, z: 4, core: 2. Of those that a mesh axis runs over, the one named last changes fastest.
Arguments:
- residual_in: bfloat16 [64, 2560], P(('dp', 'tensor')), may hold values from -6 to 6
- norm_gain: bfloat16 [2560], replicated, may hold values from 0.099609375 to 1.8984375
- w_query: bfloat16 [2560, 2560], P(None, 'tensor'), may hold values from -0.125 to 0.125
- key_weight: bfloat16 [2560, 640], P(None, 'tensor'), may hold values from -0.125 to 0.125
- value_weight: bfloat16 [2560, 640], P(None, 'tensor'), may hold values from -0.125 to 0.125
- key_page_pool: bfloat16 [256, 8, 80, 128], P('dp', 'tensor')
- value_page_pool: bfloat16 [256, 8, 80, 128], P('dp', 'tensor'), may hold values from -6 to 6
- lengths: int32 [64], replicated, may hold values from 1 to 512, as said below
- page_table: int32 [64, 4], replicated, may hold values from 0 to 255, as said below
- w_output: bfloat16 [2560, 2560], P('tensor'), may hold values from -0.125 to 0.125
- mlp_gain: bfloat16 [2560], replicated, may hold values from 0.099609375 to 1.8984375
- w_gate: bfloat16 [2560, 3584], P(None, 'tensor'), may hold values from -0.125 to 0.125
- w_up: bfloat16 [2560, 3584], P(None, 'tensor'), may hold values from -0.125 to 0.125
- w_down: bfloat16 [3584, 2560], P('tensor'), may hold values from -0.09375 to 0.09375
Outputs:
- residual_out: bfloat16 [64, 2560], P(('dp', 'tensor'))
Inputs may be any that keep to these rules, and one draw needn't show every extreme that they name: `lengths`: every value from 1 to 512 can occur; 512 and 1 occur in every draw. `page_table`: all entries are distinct. Requests are ranked by lengths[r] * 64 + r, rising; rank k goes to serving index s = k % N where N = 8 is the number of indices of dp, or N - 1 - k % N when k // N is odd, as its (k // N)-th served request; all pages of a request lie in pool pages s * 32 to (s + 1) * 32 - 1 of its serving index; pages past a request's length hold unused data.
All inputs are finite; a program needn't handle non-finite values.
Results may differ from a plain program's by a relative error of at most 0.0096.
Values may be sent and summed in bfloat16 or wider, within the bound.
No kernel may reach another device: no remote copies, remote signals or barrier semaphores. Data moves between devices by JAX's collectives and lax.ppermute only.
A program may use at most 64 MiB of HBM per device.

v0:
```python
import jax
import jax.numpy as jnp
from jax import lax
from jax.sharding import PartitionSpec as P

HEAD_SIZE = 80


def norm_rows(value_rows, gain):
    value_rows = value_rows.astype(jnp.float32)
    return (
        value_rows
        * lax.rsqrt(jnp.mean(value_rows * value_rows, axis=-1, keepdims=True) + 1e-05)
        * gain.astype(jnp.float32)
    )


def apply_rotation(tensor, positions):
    half_dim = tensor.shape[-1] // 2
    inverse_freq = 1000000.0 ** (
        -(jnp.arange(half_dim, dtype=jnp.float32) * 2.0 / tensor.shape[-1])
    )
    angles = positions.astype(jnp.float32)[:, None] * inverse_freq[None, :]
    cosine = jnp.cos(angles)[:, None, :]
    sines = jnp.sin(angles)[:, None, :]
    first_half = tensor[..., :half_dim]
    second_half = tensor[..., half_dim:]
    return jnp.concatenate(
        [first_half * cosine - second_half * sines, second_half * cosine + first_half * sines],
        axis=-1,
    )


def local(
    residual_in,
    norm_gain,
    w_query,
    key_weight,
    value_weight,
    key_page_pool,
    value_page_pool,
    lengths,
    page_table,
    w_output,
    mlp_gain,
    w_gate,
    w_up,
    w_down,
):
    dp_count = lax.axis_size("dp")
    tp_count = lax.axis_size("tensor")
    rows_loc = residual_in.shape[0]
    req_loc = rows_loc * tp_count
    kv_loc = key_page_pool.shape[1]
    q_loc = w_query.shape[1] // HEAD_SIZE
    group_width = q_loc // kv_loc
    pool_size = key_page_pool.shape[0]
    page_len = key_page_pool.shape[3]
    per_req = page_table.shape[1]
    total_reqs = page_table.shape[0]
    score_scale = 1.0 / HEAD_SIZE**0.5
    dp_index = lax.axis_index("dp")
    rows_all = lax.all_gather(residual_in, "tensor", axis=0, tiled=True)
    scaled_input = norm_rows(rows_all, norm_gain).astype(jnp.bfloat16)
    first_row = dp_index * req_loc
    own_len = lax.dynamic_slice_in_dim(lengths, first_row, req_loc, 0)
    query_heads = apply_rotation(
        jnp.dot(scaled_input, w_query, preferred_element_type=jnp.float32).reshape(
            req_loc, q_loc, HEAD_SIZE
        ),
        own_len,
    ).astype(jnp.bfloat16)
    fresh_key = apply_rotation(
        jnp.dot(scaled_input, key_weight, preferred_element_type=jnp.float32).reshape(
            req_loc, kv_loc, HEAD_SIZE
        ),
        own_len,
    ).astype(jnp.bfloat16)
    fresh_value = (
        jnp.dot(scaled_input, value_weight, preferred_element_type=jnp.float32)
        .astype(jnp.bfloat16)
        .reshape(req_loc, kv_loc, HEAD_SIZE)
    )
    request_ids = jnp.arange(total_reqs, dtype=jnp.int32)
    ranking = lengths * total_reqs + request_ids
    order = jnp.argsort(ranking, stable=True)
    rank = jnp.argsort(order, stable=True)
    round_no = rank // dp_count
    column = rank % dp_count
    server = jnp.where(round_no % 2 == 0, column, dp_count - 1 - column)
    slot_of = server * req_loc + round_no
    my_slots = first_row + jnp.arange(req_loc, dtype=jnp.int32)
    hits = (slot_of[None, :] == my_slots[:, None]).astype(jnp.int32)
    served = jnp.sum(hits * request_ids[None, :], axis=1)
    query_all, key_all, value_all = (
        lax.all_gather(query_heads.reshape(req_loc, q_loc * HEAD_SIZE), "dp", axis=0, tiled=True),
        lax.all_gather(fresh_key.reshape(req_loc, kv_loc * HEAD_SIZE), "dp", axis=0, tiled=True),
        lax.all_gather(fresh_value.reshape(req_loc, kv_loc * HEAD_SIZE), "dp", axis=0, tiled=True),
    )
    query_srv = query_all[served].reshape(req_loc, kv_loc, group_width, HEAD_SIZE)
    key_srv = key_all[served].reshape(req_loc, kv_loc, HEAD_SIZE)
    value_srv = value_all[served].reshape(req_loc, kv_loc, HEAD_SIZE)
    page_list = page_table[served] - dp_index * pool_size
    key_rows = key_page_pool[page_list]
    value_rows = value_page_pool[page_list]
    scores = (
        jnp.einsum("rhgd,rphdc->rhgpc", query_srv, key_rows, preferred_element_type=jnp.float32)
        * score_scale
    )
    positions = (
        jnp.arange(per_req, dtype=jnp.int32)[:, None] * page_len
        + jnp.arange(page_len, dtype=jnp.int32)[None, :]
    )
    valid_pos = (positions[None, :, :] < lengths[served][:, None, None])[:, None, None, :, :]
    own_score = (
        jnp.einsum("rhgd,rhd->rhg", query_srv, key_srv, preferred_element_type=jnp.float32)
        * score_scale
    )
    best = jnp.maximum(jnp.max(jnp.where(valid_pos, scores, -1e30), axis=(-2, -1)), own_score)
    weights = jnp.where(valid_pos, jnp.exp(scores - best[..., None, None]), 0.0)
    own_weight = jnp.exp(own_score - best)
    numer = (
        jnp.einsum("rhgpc,rphdc->rhgd", weights, value_rows.astype(jnp.float32))
        + own_weight[..., None] * value_srv.astype(jnp.float32)[:, :, None, :]
    )
    denom = jnp.sum(weights, axis=(-2, -1)) + own_weight
    served_out = (numer / denom[..., None]).reshape(req_loc, q_loc * HEAD_SIZE).astype(jnp.bfloat16)
    every_out = lax.all_gather(served_out, "dp", axis=0, tiled=True)
    attended = every_out[lax.dynamic_slice_in_dim(slot_of, first_row, req_loc, 0)]
    summed = lax.psum(jnp.dot(attended, w_output, preferred_element_type=jnp.float32), "tensor")
    mixed_all = rows_all.astype(jnp.float32) + summed
    normed_mlp = norm_rows(mixed_all, mlp_gain).astype(jnp.bfloat16)
    mixed = lax.dynamic_slice_in_dim(mixed_all, lax.axis_index("tensor") * rows_loc, rows_loc, 0)
    gate_act = jnp.dot(normed_mlp, w_gate, preferred_element_type=jnp.float32)
    up_act = jnp.dot(normed_mlp, w_up, preferred_element_type=jnp.float32)
    hidden = (jax.nn.silu(gate_act) * up_act).astype(jnp.bfloat16)
    down_part = lax.psum_scatter(
        jnp.dot(hidden, w_down, preferred_element_type=jnp.float32),
        "tensor",
        scatter_dimension=0,
        tiled=True,
    )
    return (mixed + down_part).astype(jnp.bfloat16)


def solution(mesh):
    return jax.shard_map(
        local,
        mesh=mesh,
        in_specs=(
            P(("dp", "tensor"), None),
            P(),
            P(None, "tensor"),
            P(None, "tensor"),
            P(None, "tensor"),
            P("dp", "tensor", None, None),
            P("dp", "tensor", None, None),
            P(),
            P(),
            P("tensor", None),
            P(),
            P(None, "tensor"),
            P(None, "tensor"),
            P("tensor", None),
        ),
        out_specs=P(("dp", "tensor"), None),
        check_vma=False,
    )
```

profile of v0, /device:TPU:0, one launch (start us, length us, event | category | flops | bytes accessed | tf_op | source)
XLA Modules:
  0.0 175.6 jit_solution(13523892685238837358)
XLA Ops:
  6.6 0.8 iota_add_fusion.2
  7.4 0.9 dynamic-slice_convert_fusion
  8.3 15.0 %all-gather = bf16[4,2,2560]{2,1,0:T(2,128)(2,1)S(1)} all-gather(bf16[1,2,2560]{2,1,0:T(2,128)(2,1)} %bitcast.45), channel_id=1, replica_groups=mesh['dp'=8,'tensor'=4] {'tensor'}, dimensions={0}, use_global_device_ids=true | all-gather | bytes 51200 | tf_op jit(solution)/shard_map/all_gather | solution.py:63
  23.4 0.7 convert_element_type.58
  24.2 2.5 %fusion.39 = f32[8,640]{1,0:T(8,128)S(1)} fusion(bf16[8,2560]{1,0:T(8,128)(2,1)S(1)} %multiply_convert_fusion.1, bf16[2560,640]{1,0:T(8,128)(2,1)} %param.16), kind=kOutput, calls=%fused_computation.83 | convolution fusion | flops 26214400 | bytes 3338240 | tf_op jit(solution)/shard_map/dot_general | solution.py:68
  27.1 9.3 %all_gather.16 = bf16[64,640]{1,0:T(8,128)(2,1)S(1)} all-gather(bf16[8,640]{1,0:T(8,128)(2,1)S(1)} %convert_element_type.61), channel_id=1, replica_groups=mesh['dp'=8,'tensor'=4] {'dp'}, dimensions={0}, use_global_device_ids=true | all-gather | bytes 92160 | tf_op jit(solution)/shard_map/all_gather | solution.py:96
  36.4 2.0 %sort.31 = (s32[64]{0:T(128)}, s32[64]{0:T(128)S(1)}) sort(s32[64]{0:T(128)S(1)} %iota_add_fusion.2, s32[64]{0:T(128)S(1)} %iota.39), dimensions={0}, to_apply=%region_0.0 | sort | flops 384 | bytes 1024 | tf_op jit(solution)/shard_map/jit(argsort)/sort | solution.py:86
  38.4 2.0 %sort.32 = (s32[64]{0:T(128)}, s32[64]{0:T(128)S(1)}) sort(s32[64]{0:T(128)S(1)} %get-tuple-element.7, s32[64]{0:T(128)S(1)} %iota.40), dimensions={0}, to_apply=%region_1.0 | sort | flops 384 | bytes 1024 | tf_op jit(solution)/shard_map/jit(argsort)/sort | solution.py:87
  43.4 1.4 fusion.40
  45.2 9.0 %all_gather.17 = bf16[64,160]{1,0:T(8,128)(2,1)S(1)} all-gather(bf16[8,160]{1,0:T(8,128)(2,1)S(1)} %convert_element_type.62), channel_id=1, replica_groups=mesh['dp'=8,'tensor'=4] {'dp'}, dimensions={0}, use_global_device_ids=true | all-gather | bytes 23040 | tf_op jit(solution)/shard_map/all_gather | solution.py:97
  56.0 3.1 %gather_fusion.3 = bf16[32,2,80,128]{3,2,1,0:T(8,128)(2,1)} fusion(bf16[32,2,80,128]{3,2,1,0:T(8,128)(2,1)} %param.19, s32[1024]{0:T(1024)S(1)} %pad_clamp_fusion.1), kind=kCustom, calls=%fused_computation.3 | custom fusion | bytes 2621568 | tf_op jit(solution)/shard_map/gather | solution.py:104
  59.2 1.7 select_reduce_fusion
  61.8 1.5 convolution_convert_fusion
  63.2 8.1 %all_gather.18 = bf16[64,160]{1,0:T(8,128)(2,1)S(1)} all-gather(bf16[8,160]{1,0:T(8,128)(2,1)S(1)} %convolution_convert_fusion), channel_id=1, replica_groups=mesh['dp'=8,'tensor'=4] {'dp'}, dimensions={0}, use_global_device_ids=true | all-gather | bytes 23040 | tf_op jit(solution)/shard_map/all_gather | solution.py:98
  72.1 3.1 %gather_fusion.5 = bf16[32,2,80,128]{3,2,1,0:T(8,128)(2,1)} fusion(bf16[32,2,80,128]{3,2,1,0:T(8,128)(2,1)} %param.20, s32[1024]{0:T(1024)S(1)} %pad_clamp_fusion.1), kind=kCustom, calls=%fused_computation.5 | custom fusion | bytes 2621568 | tf_op jit(solution)/shard_map/gather | solution.py:105
  75.2 1.8 %fusion.16 = bf16[8,2,4,80]{3,2,1,0:T(4,128)(2,1)S(1)} fusion(bf16[8,4,2,80,128]{4,3,2,1,0:T(8,128)(2,1)} %bitcast.41, f32[8,2,4,4,128]{4,2,3,1,0:T(4,128)S(1)} %get-tuple-element.20, f32[8,2,4]{2,1,0:T(2,128)S(1)} %multiply_maximum_fusion, pred[8,4,128]{2,1,0:T(4,128)(4,1)S(1)} %broadcast_compare_fusion, f32[8,2,4]{2,1,0:T(2,128)S(1)} %copy-done.3, ...), kind=kOutput, calls=%fused_computation.17 | convolution fusion | flops 5328896 | bytes 1462016 | tf_op jit(solution)/shard_map/rhgpc,rphdc->rhgd/dot_general | solution.py:123
  77.1 9.2 %all_gather.19 = bf16[64,640]{1,0:T(8,128)(2,1)S(1)} all-gather(bf16[8,640]{1,0:T(8,128)(2,1)S(1)} %convert_element_type.67), channel_id=1, replica_groups=mesh['dp'=8,'tensor'=4] {'dp'}, dimensions={0}, use_global_device_ids=true | all-gather | bytes 92160 | tf_op jit(solution)/shard_map/all_gather | solution.py:128
  87.6 1.2 fusion.42
  89.6 33.5 %all-reduce.4.cloned.1.call-done = f32[8,2560]{1,0:T(8,128)} async-done(((f32[8,2560]{1,0:T(8,128)}), f32[8,2560]{1,0:T(8,128)}) %all-reduce.4.cloned.1.call-update) | async-done | bytes 81936 | tf_op jit(solution)/shard_map/psum | solution.py:130
  123.1 1.0 multiply_reduce_fusion
  124.1 3.0 %fusion.37 = f32[8,896]{1,0:T(8,128)S(1)} fusion(bf16[2560,896]{1,0:T(8,128)(2,1)} %param.25, f32[8,2560]{1,0:T(8,128)S(1)} %get-tuple-element.10, f32[2560]{0:T(1024)S(1)} %convert_element_type.68, f32[8]{0:T(128)S(1)} %add_rsqrt_fusion), kind=kOutput, calls=%fused_computation.81 | convolution fusion | flops 36761600 | bytes 4708384 | tf_op jit(solution)/shard_map/dot_general | solution.py:134
  127.2 5.9 %fusion.20 = f32[8,2560]{1,0:T(8,128)} fusion(bf16[896,2560]{1,0:T(8,128)(2,1)} %param.27, bf16[2560,896]{1,0:T(8,128)(2,1)} %param.26, f32[8,896]{1,0:T(8,128)S(1)} %fusion.37, f32[8,2560]{1,0:T(8,128)S(1)} %get-tuple-element.10, f32[2560]{0:T(1024)S(1)} %convert_element_type.68, f32[8]{0:T(128)S(1)} %add_rsqrt_fusion), kind=kOutput, calls=%fused_computation.19 | convolution fusion | flops 73504768 | bytes 9377824 | tf_op jit(solution)/shard_map/dot_general | solution.py:138
  134.4 32.9 %all-reduce.6.cloned.1.call-done = f32[8,2560]{1,0:T(8,128)} async-done(((f32[8,2560]{1,0:T(8,128)}), f32[8,2560]{1,0:T(8,128)}) %all-reduce.6.cloned.1.call-update) | async-done | bytes 81936
  167.2 1.5 fusion.30
  (67 shorter events, 10.1 us)
Async XLA Ops:
  6.5 81.1 %copy-start = (bf16[640,2560]{1,0:T(8,128)(2,1)S(1)}, bf16[640,2560]{1,0:T(8,128)(2,1)}, u32[]{:S(2)}) copy-start(bf16[640,2560]{1,0:T(8,128)(2,1)} %param.23) | copy-start | bytes 9830404
  6.5 35.5 %copy-start.1 = (s32[64]{0:T(128)S(1)}, s32[64]{0:T(128)}, u32[]{:S(2)}) copy-start(s32[64]{0:T(128)} %param.21) | copy-start | bytes 772
  6.5 48.3 %copy-start.4 = (s32[64,4]{0,1:T(4,128)S(1)}, s32[64,4]{0,1:T(4,128)}, u32[]{:S(2)}) copy-start(s32[64,4]{0,1:T(4,128)} %param.22) | copy-start | bytes 3076
  6.5 116.5 %all-reduce.4.cloned.1.call-start = ((), (), s32[]{:S(2)}) async-start(), calls=%async_computation | async-start | bytes 163840 | tf_op jit(solution)/shard_map/psum | solution.py:130
  40.7 18.5 %copy-start.2 = (s32[1024]{0:T(1024)}, s32[1024]{0:T(1024)S(1)}, u32[]{:S(2)}) copy-start(s32[1024]{0:T(1024)S(1)} %pad_clamp_fusion.2) | copy-start | bytes 12292
  61.8 13.4 %copy-start.3 = (f32[8,2,4]{2,1,0:T(2,128)S(1)}, f32[8,2,4]{2,1,0:T(2,128)}, u32[]{:S(2)}) copy-start(f32[8,2,4]{2,1,0:T(2,128)} %get-tuple-element.11) | copy-start | bytes 772
  88.8 78.4 %all-reduce.6.cloned.1.call-start = ((), (), s32[]{:S(2)}) async-start(), calls=%async_computation.1 | async-start | bytes 163840
  127.1 6.0 %copy-start.5 = (u32[32]{0:T(128)S(1)}, u32[32]{0:T(128)}, u32[]{:S(2)}) copy-start(u32[32]{0:T(128)} %constant.93) | copy-start | bytes 388
Sparse Core Ops, SparseCore 0:
  88.9 34.0 all-reduce.3
  133.2 33.9 all-reduce.5
where the time goes:
time: 176 us
  waiting for transfers between devices  66.4 us (38%)
  blocking collectives  50.7 us (29%)
  matrix products  19.1 us (11%)
  between operations  14.2 us (8%)
  other arithmetic  13 us (7%)
  local copies, waits for them, and re-layouts  12.2 us (7%)
    psum x1, waiting for transfers between devices, local(): lax.psum(jnp.dot(attended, w_output, preferred_element_type=jnp.float32),...  33.5 us
    unnamed x3, waiting for transfers between devices  32.9 us
    all_gather x1, blocking collectives, local(): rows_all = lax.all_gather(residual_in, 'tensor', axis=0, tiled=True)  15 us
    all_gather x1, blocking collectives, local(): lax.all_gather(query_heads.reshape(req_loc, q_loc * HEAD_SIZE), 'dp', axi...  9.27 us
    all_gather x1, blocking collectives, local(): every_out = lax.all_gather(served_out, 'dp', axis=0, tiled=True)  9.24 us
    all_gather x1, blocking collectives, local(): lax.all_gather(fresh_key.reshape(req_loc, kv_loc * HEAD_SIZE), 'dp', axis...  9.03 us
    all_gather x1, blocking collectives, local(): lax.all_gather(fresh_value.reshape(req_loc, kv_loc * HEAD_SIZE), 'dp', ax...  8.12 us
    dot_general x1, matrix products, local(): jnp.dot(hidden, w_down, preferred_element_type=jnp.float32)  5.93 us
  transfers between devices with their start and end apart: 2, of which 2 were waited for; matrix products, arithmetic and copies ran while one was open for 1% of the time, Pallas kernels for 0%

commit v1 on v0

--- a/solution.py
+++ b/solution.py
@@ -127,7 +127,10 @@
     served_out = (numer / denom[..., None]).reshape(req_loc, q_loc * HEAD_SIZE).astype(jnp.bfloat16)
     every_out = lax.all_gather(served_out, "dp", axis=0, tiled=True)
     attended = every_out[lax.dynamic_slice_in_dim(slot_of, first_row, req_loc, 0)]
-    summed = lax.psum(jnp.dot(attended, w_output, preferred_element_type=jnp.float32), "tensor")
+    summed = jnp.sum(
+        lax.all_gather(jnp.dot(attended, w_output, preferred_element_type=jnp.float32), "tensor"),
+        axis=0,
+    )
     mixed_all = rows_all.astype(jnp.float32) + summed
     normed_mlp = norm_rows(mixed_all, mlp_gain).astype(jnp.bfloat16)
     mixed = lax.dynamic_slice_in_dim(mixed_all, lax.axis_index("tensor") * rows_loc, rows_loc, 0)

time: 176 us -> 156 us (0.89)
  waiting for transfers between devices: 66.4 us -> 33.7 us
  blocking collectives: 50.7 us -> 65 us
    psum x1 -> x0, waiting for transfers between devices: 33.5 us -> none  [local(): lax.psum(jnp.dot(attended, w_output, preferred_element_type=jnp.float32),...]
    all_gather x0 -> x1, blocking collectives: none -> 14.4 us  [local(): lax.all_gather(jnp.dot(attended, w_output, preferred_element_type=jnp.flo...]
    unnamed x3 -> x2, waiting for transfers between devices: 32.9 us -> 33.7 us
  transfers between devices with their start and end apart: 2 -> 1, of which waited for: 2 -> 1; matrix products, arithmetic and copies ran while one was open for 1% -> 0% of each run, Pallas kernels for 0% -> 0%
where the time goes in v1:
time: 156 us; the launch traced here: 155 us
  blocking collectives  65 us (42%)
  waiting for transfers between devices  33.7 us (22%)
  matrix products  18.5 us (12%)
  between operations  14.2 us (9%)
  local copies, waits for them, and re-layouts  12.2 us (8%)
  other arithmetic  11.4 us (7%)
    unnamed x2, waiting for transfers between devices  33.7 us
    all_gather x1, blocking collectives, local(): rows_all = lax.all_gather(residual_in, 'tensor', axis=0, tiled=True)  15 us
    all_gather x1, blocking collectives, local(): lax.all_gather(jnp.dot(attended, w_output, preferred_element_type=jnp.flo...  14.4 us
    all_gather x1, blocking collectives, local(): lax.all_gather(query_heads.reshape(req_loc, q_loc * HEAD_SIZE), 'dp', axi...  9.27 us
    all_gather x1, blocking collectives, local(): every_out = lax.all_gather(served_out, 'dp', axis=0, tiled=True)  9.24 us
    all_gather x1, blocking collectives, local(): lax.all_gather(fresh_key.reshape(req_loc, kv_loc * HEAD_SIZE), 'dp', axis...  9.03 us
    all_gather x1, blocking collectives, local(): lax.all_gather(fresh_value.reshape(req_loc, kv_loc * HEAD_SIZE), 'dp', ax...  8.12 us
    dot_general x1, matrix products, local(): jnp.dot(hidden, w_down, preferred_element_type=jnp.float32)  5.93 us
  transfers between devices with their start and end apart: 1, of which 1 were waited for; matrix products, arithmetic and copies ran while one was open for 0% of the time, Pallas kernels for 0%

profile of v1, /device:TPU:0, one launch (start us, length us, event | category | flops | bytes accessed | tf_op | source)
XLA Modules:
  0.0 155.0 jit_solution(12301773684611281850)
XLA Ops:
  6.6 0.8 iota_add_fusion.2
  7.4 0.9 dynamic-slice_convert_fusion
  8.3 15.0 %all-gather.1 = bf16[4,2,2560]{2,1,0:T(2,128)(2,1)S(1)} all-gather(bf16[1,2,2560]{2,1,0:T(2,128)(2,1)} %bitcast.47), channel_id=1, replica_groups=mesh['dp'=8,'tensor'=4] {'tensor'}, dimensions={0}, use_global_device_ids=true | all-gather | bytes 51200 | tf_op jit(solution)/shard_map/all_gather | solution.py:63
  23.4 0.7 convert_element_type.58
  24.2 2.5 %fusion.39 = f32[8,640]{1,0:T(8,128)S(1)} fusion(bf16[8,2560]{1,0:T(8,128)(2,1)S(1)} %multiply_convert_fusion.1, bf16[2560,640]{1,0:T(8,128)(2,1)} %param.16), kind=kOutput, calls=%fused_computation.84 | convolution fusion | flops 26214400 | bytes 3338240 | tf_op jit(solution)/shard_map/dot_general | solution.py:68
  27.1 9.3 %all_gather.22 = bf16[64,640]{1,0:T(8,128)(2,1)S(1)} all-gather(bf16[8,640]{1,0:T(8,128)(2,1)S(1)} %convert_element_type.61), channel_id=1, replica_groups=mesh['dp'=8,'tensor'=4] {'dp'}, dimensions={0}, use_global_device_ids=true | all-gather | bytes 92160 | tf_op jit(solution)/shard_map/all_gather | solution.py:96
  36.4 2.0 %sort.31 = (s32[64]{0:T(128)}, s32[64]{0:T(128)S(1)}) sort(s32[64]{0:T(128)S(1)} %iota_add_fusion.2, s32[64]{0:T(128)S(1)} %iota.39), dimensions={0}, to_apply=%region_0.0 | sort | flops 384 | bytes 1024 | tf_op jit(solution)/shard_map/jit(argsort)/sort | solution.py:86
  38.4 2.0 %sort.32 = (s32[64]{0:T(128)}, s32[64]{0:T(128)S(1)}) sort(s32[64]{0:T(128)S(1)} %get-tuple-element.7, s32[64]{0:T(128)S(1)} %iota.40), dimensions={0}, to_apply=%region_1.0 | sort | flops 384 | bytes 1024 | tf_op jit(solution)/shard_map/jit(argsort)/sort | solution.py:87
  41.4 0.7 reshape.238
  43.4 1.4 fusion.40
  45.2 9.0 %all_gather.23 = bf16[64,160]{1,0:T(8,128)(2,1)S(1)} all-gather(bf16[8,160]{1,0:T(8,128)(2,1)S(1)} %convert_element_type.62), channel_id=1, replica_groups=mesh['dp'=8,'tensor'=4] {'dp'}, dimensions={0}, use_global_device_ids=true | all-gather | bytes 23040 | tf_op jit(solution)/shard_map/all_gather | solution.py:97
  56.0 3.1 %gather_fusion.3 = bf16[32,2,80,128]{3,2,1,0:T(8,128)(2,1)} fusion(bf16[32,2,80,128]{3,2,1,0:T(8,128)(2,1)} %param.19, s32[1024]{0:T(1024)S(1)} %pad_clamp_fusion.1), kind=kCustom, calls=%fused_computation.3 | custom fusion | bytes 2621568 | tf_op jit(solution)/shard_map/gather | solution.py:104
  59.2 1.7 %select_reduce_fusion = (f32[8,2,4]{2,1,0:T(2,128)S(1)}, f32[8,2,4,4,128]{4,2,3,1,0:T(4,128)S(1)}) fusion(pred[8,4,128]{2,1,0:T(4,128)(4,1)S(1)} %broadcast_compare_fusion, bf16[8,4,2,80,128]{4,3,2,1,0:T(8,128)(2,1)} %bitcast.44, bf16[8,2,4,80,1]{3,2,1,0,4:T(4,128)(2,1)} %reshape.238), kind=kOutput, calls=%fused_computation.23 | convolution fusion | flops 5341120 | bytes 1456384 | tf_op jit(solution)/shard_map/rhgd,rphdc->rhgpc/dot_general | solution.py:107
  61.8 1.5 convolution_convert_fusion
  63.2 8.1 %all_gather.24 = bf16[64,160]{1,0:T(8,128)(2,1)S(1)} all-gather(bf16[8,160]{1,0:T(8,128)(2,1)S(1)} %convolution_convert_fusion), channel_id=1, replica_groups=mesh['dp'=8,'tensor'=4] {'dp'}, dimensions={0}, use_global_device_ids=true | all-gather | bytes 23040 | tf_op jit(solution)/shard_map/all_gather | solution.py:98
  71.3 0.7 gather_fusion.6
  72.1 3.1 %gather_fusion.5 = bf16[32,2,80,128]{3,2,1,0:T(8,128)(2,1)} fusion(bf16[32,2,80,128]{3,2,1,0:T(8,128)(2,1)} %param.20, s32[1024]{0:T(1024)S(1)} %pad_clamp_fusion.1), kind=kCustom, calls=%fused_computation.5 | custom fusion | bytes 2621568 | tf_op jit(solution)/shard_map/gather | solution.py:105
  75.2 1.8 %fusion.16 = bf16[8,2,4,80]{3,2,1,0:T(4,128)(2,1)S(1)} fusion(bf16[8,4,2,80,128]{4,3,2,1,0:T(8,128)(2,1)} %bitcast.43, f32[8,2,4,4,128]{4,2,3,1,0:T(4,128)S(1)} %get-tuple-element.20, f32[8,2,4]{2,1,0:T(2,128)S(1)} %multiply_maximum_fusion, pred[8,4,128]{2,1,0:T(4,128)(4,1)S(1)} %broadcast_compare_fusion, f32[8,2,4]{2,1,0:T(2,128)S(1)} %copy-done.3, ...), kind=kOutput, calls=%fused_computation.17 | convolution fusion | flops 5328896 | bytes 1462016 | tf_op jit(solution)/shard_map/rhgpc,rphdc->rhgd/dot_general | solution.py:123
  77.1 9.2 %all_gather.25 = bf16[64,640]{1,0:T(8,128)(2,1)S(1)} all-gather(bf16[8,640]{1,0:T(8,128)(2,1)S(1)} %convert_element_type.67), channel_id=1, replica_groups=mesh['dp'=8,'tensor'=4] {'dp'}, dimensions={0}, use_global_device_ids=true | all-gather | bytes 92160 | tf_op jit(solution)/shard_map/all_gather | solution.py:128
  88.2 14.4 %all-gather = f32[32,2560]{1,0:T(8,128)S(1)} all-gather(f32[8,2560]{1,0:T(8,128)S(1)} %fusion.42), channel_id=2, replica_groups=mesh['dp'=8,'tensor'=4] {'tensor'}, dimensions={0}, use_global_device_ids=true | all-gather | bytes 409600 | tf_op jit(solution)/shard_map/all_gather | solution.py:131
  102.7 3.0 %fusion.37 = f32[8,896]{1,0:T(8,128)S(1)} fusion(bf16[2560,896]{1,0:T(8,128)(2,1)} %param.25, f32[8,2560]{1,0:T(8,128)S(1)} %get-tuple-element.10, f32[2560]{0:T(1024)S(1)} %convert_element_type.68, f32[8]{0:T(128)S(1)} %add_rsqrt_fusion), kind=kOutput, calls=%fused_computation.82 | convolution fusion | flops 36761600 | bytes 4708384 | tf_op jit(solution)/shard_map/dot_general | solution.py:137
  105.7 5.9 %fusion.20 = f32[8,2560]{1,0:T(8,128)} fusion(bf16[896,2560]{1,0:T(8,128)(2,1)} %param.27, bf16[2560,896]{1,0:T(8,128)(2,1)} %param.26, f32[8,896]{1,0:T(8,128)S(1)} %fusion.37, f32[8,2560]{1,0:T(8,128)S(1)} %get-tuple-element.10, f32[2560]{0:T(1024)S(1)} %convert_element_type.68, f32[8]{0:T(128)S(1)} %add_rsqrt_fusion), kind=kOutput, calls=%fused_computation.19 | convolution fusion | flops 73504768 | bytes 9377824 | tf_op jit(solution)/shard_map/dot_general | solution.py:141
  112.9 33.7 %all-reduce.3.cloned.1.call-done = f32[8,2560]{1,0:T(8,128)} async-done(((f32[8,2560]{1,0:T(8,128)}), f32[8,2560]{1,0:T(8,128)}) %all-reduce.3.cloned.1.call-update) | async-done | bytes 81936
  146.6 1.5 fusion.30
  (68 shorter events, 8.7 us)
Async XLA Ops:
  6.5 81.1 %copy-start = (bf16[640,2560]{1,0:T(8,128)(2,1)S(1)}, bf16[640,2560]{1,0:T(8,128)(2,1)}, u32[]{:S(2)}) copy-start(bf16[640,2560]{1,0:T(8,128)(2,1)} %param.23) | copy-start | bytes 9830404
  6.5 35.5 %copy-start.1 = (s32[64]{0:T(128)S(1)}, s32[64]{0:T(128)}, u32[]{:S(2)}) copy-start(s32[64]{0:T(128)} %param.21) | copy-start | bytes 772
  6.5 48.3 %copy-start.5 = (s32[64,4]{0,1:T(4,128)S(1)}, s32[64,4]{0,1:T(4,128)}, u32[]{:S(2)}) copy-start(s32[64,4]{0,1:T(4,128)} %param.22) | copy-start | bytes 3076
  6.5 140.1 %all-reduce.3.cloned.1.call-start = ((), (), s32[]{:S(2)}) async-start(), calls=%async_computation | async-start | bytes 163840
  40.7 18.5 %copy-start.2 = (s32[1024]{0:T(1024)}, s32[1024]{0:T(1024)S(1)}, u32[]{:S(2)}) copy-start(s32[1024]{0:T(1024)S(1)} %pad_clamp_fusion.2) | copy-start | bytes 12292
  61.8 13.4 %copy-start.3 = (f32[8,2,4]{2,1,0:T(2,128)S(1)}, f32[8,2,4]{2,1,0:T(2,128)}, u32[]{:S(2)}) copy-start(f32[8,2,4]{2,1,0:T(2,128)} %get-tuple-element.11) | copy-start | bytes 772
  77.0 25.7 %copy-start.4 = (bf16[2560]{0:T(1024)(128)(2,1)S(1)}, bf16[2560]{0:T(1024)(128)(2,1)}, u32[]{:S(2)}) copy-start(bf16[2560]{0:T(1024)(128)(2,1)} %param.24) | copy-start | bytes 15364
  105.7 6.0 %copy-start.6 = (u32[32]{0:T(128)S(1)}, u32[32]{0:T(128)}, u32[]{:S(2)}) copy-start(u32[32]{0:T(128)} %constant.93) | copy-start | bytes 388
Sparse Core Ops, SparseCore 0:
  111.8 34.7 all-reduce.2
